TPU v7x, 512 devices: a whole 4x8x8 slice. The times are simulated.
512 devices in a mesh: dp: 8 (over z), expert: 64 (over y, x, core).
Axes of the slice: x: 4, y: 8, z: 8, core: 2. Of those that a mesh axis runs over, the one named last changes fastest.
Arguments:
- query: bfloat16 [128, 8192], P('dp'), may hold values from -1200 to 1200
- new_kv: bfloat16 [128, 1024], P('dp'), may hold values from -5 to 5
- kv_cache: bfloat16 [128, 1024, 1024], P('dp', 'expert'), may hold values from -6 to 6
- lengths: int32 [128], P('dp'), may hold values from 2 to 1024, as said below
- fork_parent: int32 [64], replicated, may hold values from 0 to 127, as said below
- fork_child: int32 [64], replicated, may hold values from 0 to 126, as said below
- fork_block: int32 [64], replicated, may hold values from 0 to 63, as said below
- out_weight: bfloat16 [8192, 4096], P('expert'), may hold values from -1 to 1
- residual: bfloat16 [128, 4096], P('dp'), may hold values from -300 to 300
- route_ids: int32 [128, 8], replicated, may hold values from 0 to 63, all different within a row; in each aligned block of 16 rows (0 to 15, 16 to 31, ...) at most 4 rows name the same one
- route_weights: float32 [128, 8], replicated, may hold values from 0.02 to 0.3
- w_gate: bfloat16 [64, 4096, 1024], P('expert', None, 'dp'), may hold values from -0.09375 to 0.09375
- w_up: bfloat16 [64, 4096, 1024], P('expert', None, 'dp'), may hold values from -0.09375 to 0.09375
- w_down: bfloat16 [64, 1024, 4096], P('expert', 'dp'), may hold values from -0.1875 to 0.1875
Outputs:
- attn_proj: bfloat16 [128, 4096], P('dp', 'expert')
- expert_mix: bfloat16 [128, 4096], P('dp', 'expert')
Inputs may be any that keep to these rules, and one draw needn't show every extreme that they name: `lengths`: at least 2; a fork's child has its parent's length. `fork_parent`: fork g * 8 + d takes its parent from the branches g * 16 to (g + 1) * 16 - 1 and its child from d * 16 to (d + 1) * 16 - 1; parents are distinct, children are distinct, and no child is a parent. `fork_child`: see fork_parent. `fork_block`: at most the block that holds the parent's last cached position, (lengths - 1) // 16. `route_ids`: in each aligned block of 16 rows no expert is named by more than 4 rows, a bound that some block reaches.
All inputs are finite; a program needn't handle non-finite values.
Results may differ from a plain program's by a relative error of at most 0.024.
Values may be sent and summed in bfloat16 or wider, within the bound.
No kernel may reach another device: no remote copies, remote signals or barrier semaphores. Data moves between devices by JAX's collectives and lax.ppermute only.
A program may use at most 128 MiB of HBM per device.

v0:
```python
import math
import jax
import jax.numpy as jnp
from jax import lax
from jax.sharding import PartitionSpec as P

HD = 128
KVH = 4


def combined_all(array, axis, join):
    gathered = jax.tree.map(
        lambda a, kind: lax.all_gather(a.astype(kind), axis),
        array,
        (jnp.bfloat16, jnp.bfloat16, jnp.bfloat16),
    )

    def take(source):
        return jax.tree.map(
            lambda a, own: lax.dynamic_index_in_dim(a, source, 0, False).astype(own.dtype),
            gathered,
            array,
        )

    return lax.fori_loop(
        1, lax.axis_size(axis), lambda source, state: join(state, take(source)), take(0)
    )


def combine_parts(first, second):
    out_first, peak_first, sum_first = first
    out_second, peak_second, sum_second = second
    highest = jnp.maximum(peak_first, peak_second)
    factor_first = jnp.exp(peak_first - highest)
    factor_second = jnp.exp(peak_second - highest)
    merged_out = out_first * factor_first[..., None] + out_second * factor_second[..., None]
    return (merged_out, highest, sum_first * factor_first + sum_second * factor_second)


def shards(
    query,
    new_kv,
    kv_cache,
    lengths,
    fork_parent,
    fork_child,
    fork_block,
    out_weight,
    residual,
    route_ids,
    route_weights,
    w_gate,
    w_up,
    w_down,
):
    groups = lax.axis_size("dp")
    owners = lax.axis_size("expert")
    group_index = lax.axis_index("dp")
    owner_index = lax.axis_index("expert")
    local_rows = query.shape[0]
    positions_dev = kv_cache.shape[1]
    key_width = KVH * HD
    head_count = query.shape[1] // HD
    grouping = head_count // KVH
    own_heads = head_count // owners
    model_width = residual.shape[1]
    columns = model_width // owners
    outgoing = (
        lax.dynamic_slice_in_dim(fork_parent, group_index * groups, groups)
        - group_index * local_rows
    )
    out_blocks = lax.dynamic_slice_in_dim(fork_block, group_index * groups, groups)
    send_rows = jnp.where(
        (owner_index >= out_blocks)[:, None, None],
        kv_cache[outgoing],
        jnp.zeros((), kv_cache.dtype),
    )
    arrived = lax.all_to_all(send_rows, "dp", split_axis=0, concat_axis=0, tiled=True)
    incoming = jnp.arange(groups, dtype=jnp.int32) * groups + group_index
    targets = fork_child[incoming] - group_index * local_rows
    take_new = owner_index >= fork_block[incoming]
    cache = kv_cache.at[targets].set(jnp.where(take_new[:, None, None], arrived, kv_cache[targets]))
    score_scale = 1.0 / math.sqrt(HD)
    positions = owner_index * positions_dev + jnp.arange(positions_dev, dtype=jnp.int32)
    visible = positions[None, :] < lengths[:, None]
    cached_keys = cache[:, :, :key_width].reshape(local_rows, positions_dev, KVH, HD)
    cached_values = cache[:, :, key_width:].reshape(local_rows, positions_dev, KVH, HD)
    grouped = query.reshape(local_rows, KVH, grouping, HD)
    scores = (
        jnp.einsum("bkgd,bpkd->bkgp", grouped, cached_keys, preferred_element_type=jnp.float32)
        * score_scale
    )
    scores = jnp.where(visible[:, None, None, :], scores, -1e30)
    highest = jnp.max(scores, axis=3)
    weights = jnp.where(visible[:, None, None, :], jnp.exp(scores - highest[..., None]), 0.0)
    weight_sum = jnp.sum(weights, axis=3)
    partial_out = jnp.einsum(
        "bkgp,bpkd->bkgd",
        weights.astype(jnp.bfloat16),
        cached_values,
        preferred_element_type=jnp.float32,
    )
    partial_out = partial_out.reshape(local_rows, head_count, HD)
    highest = highest.reshape(local_rows, head_count)
    weight_sum = weight_sum.reshape(local_rows, head_count)
    merged = combined_all((partial_out, highest, weight_sum), "expert", combine_parts)
    head_out = lax.dynamic_slice_in_dim(merged[0], owner_index * own_heads, own_heads, 1)
    head_peak = lax.dynamic_slice_in_dim(merged[1], owner_index * own_heads, own_heads, 1)
    head_sum = lax.dynamic_slice_in_dim(merged[2], owner_index * own_heads, own_heads, 1)
    own_query = lax.dynamic_slice_in_dim(query, owner_index * own_heads * HD, own_heads * HD, 1)
    own_query = own_query.reshape(local_rows, own_heads, HD).astype(jnp.float32)
    kv_index = (owner_index * own_heads + jnp.arange(own_heads, dtype=jnp.int32)) // grouping
    new_keys = jnp.take(
        new_kv[:, :key_width].reshape(local_rows, KVH, HD), kv_index, axis=1
    ).astype(jnp.float32)
    new_values = jnp.take(
        new_kv[:, key_width:].reshape(local_rows, KVH, HD), kv_index, axis=1
    ).astype(jnp.float32)
    own_score = jnp.sum(own_query * new_keys, axis=2) * score_scale
    new_peak = jnp.maximum(head_peak, own_score)
    old_factor = jnp.exp(head_peak - new_peak)
    own_weight = jnp.exp(own_score - new_peak)
    denominator = head_sum * old_factor + own_weight
    own_rounded = lax.optimization_barrier(own_weight.astype(jnp.bfloat16)).astype(jnp.float32)
    attended = (
        head_out * old_factor[..., None] + own_rounded[..., None] * new_values
    ) / denominator[..., None]
    attended = attended.astype(jnp.bfloat16).reshape(local_rows, own_heads * HD)
    proj_terms = jnp.dot(attended, out_weight, preferred_element_type=jnp.float32)
    projected = lax.psum(proj_terms, "expert")
    stream = residual.astype(jnp.float32) + projected
    inverse = lax.rsqrt(jnp.sum(stream * stream, axis=1, keepdims=True) / model_width + 1e-06)
    normed = (stream * inverse).astype(jnp.bfloat16)
    attn_cols = lax.dynamic_slice_in_dim(projected, owner_index * columns, columns, 1).astype(
        jnp.bfloat16
    )
    top_k = route_ids.shape[1]
    experts_total = w_gate.shape[0] * owners
    capacity = max(2, 2 * local_rows * top_k // experts_total)
    own_ids = lax.dynamic_slice_in_dim(route_ids, group_index * local_rows, local_rows, 0)
    own_gates = lax.dynamic_slice_in_dim(route_weights, group_index * local_rows, local_rows, 0)
    matched = (own_ids == owner_index).astype(jnp.int32).reshape(-1)
    ranking = jnp.cumsum(matched) - 1
    slot_ids = jnp.arange(capacity, dtype=jnp.int32)
    onehot = ((matched[:, None] == 1) & (ranking[:, None] == slot_ids[None, :])).astype(jnp.float32)
    chosen = onehot.reshape(local_rows, top_k, capacity)
    dispatch = jnp.sum(chosen, axis=1).T
    slot_gate = jnp.sum(chosen * own_gates[:, :, None], axis=(0, 1))
    dispatch, slot_gate = (dispatch, slot_gate)
    routed = jnp.dot(
        dispatch.astype(jnp.bfloat16), normed, preferred_element_type=jnp.float32
    ).astype(jnp.bfloat16)
    piece = lax.all_gather(routed, "dp", axis=0, tiled=True)
    gate_proj = jnp.dot(piece, w_gate[0], preferred_element_type=jnp.float32)
    up_proj = jnp.dot(piece, w_up[0], preferred_element_type=jnp.float32)
    hidden = (jax.nn.silu(gate_proj) * up_proj).astype(jnp.bfloat16)
    outputs = jnp.dot(hidden, w_down[0], preferred_element_type=jnp.float32)
    summed = lax.psum_scatter(
        outputs.astype(jnp.bfloat16), "dp", scatter_dimension=0, tiled=True
    ).astype(jnp.float32)
    spread = jnp.dot(dispatch.T * slot_gate[None, :], summed, precision=lax.Precision.HIGHEST)
    mix_cols = lax.psum_scatter(spread, "expert", scatter_dimension=1, tiled=True).astype(
        jnp.bfloat16
    )
    return (attn_cols, mix_cols)


def solution(mesh):
    in_specs = (
        P("dp", None),
        P("dp", None),
        P("dp", "expert", None),
        P("dp"),
        P(),
        P(),
        P(),
        P("expert", None),
        P("dp", None),
        P(),
        P(),
        P("expert", None, "dp"),
        P("expert", None, "dp"),
        P("expert", "dp", None),
    )
    out_specs = (P("dp", "expert"), P("dp", "expert"))
    return jax.shard_map(shards, mesh=mesh, in_specs=in_specs, out_specs=out_specs, check_vma=False)
```

profile of v0, /device:TPU:16, one launch (start us, length us, event | category | flops | bytes accessed | tf_op | source)
XLA Modules:
  0.0 687.0 jit_solution(2898068980157066316)
XLA Ops:
  11.2 10.3 %all-to-all-start = ((bf16[8,16,1024]{2,1,0:T(8,128)(2,1)}), bf16[8,16,1024]{2,1,0:T(8,128)(2,1)S(1)}, u32[]{:S(2)}, u32[]{:S(2)}) async-start(bf16[8,16,1024]{2,1,0:T(8,128)(2,1)} %broadcast_select_fusion), calls=%async_computation | async-start | bytes 524288 | tf_op jit(solution)/shard_map/all_to_all | solution.py:78
  24.8 1.7 copy.82
  27.3 6.2 all-to-all-done
  40.0 39.2 %all_gather.17 = bf16[64,16,64]{2,1,0:T(8,128)(2,1)S(1)} all-gather(bf16[1,16,64]{2,1,0:T(8,128)(2,1)S(1)} %convert_element_type.161), channel_id=1, replica_groups=mesh['dp'=8,'expert'=64] {'expert'}, dimensions={0}, use_global_device_ids=true | all-gather | bytes 133120 | tf_op jit(solution)/shard_map/all_gather | solution.py:13
  79.3 37.2 %all_gather.16 = bf16[64,16,64]{2,1,0:T(8,128)(2,1)S(1)} all-gather(bf16[1,16,64]{2,1,0:T(8,128)(2,1)S(1)} %convert_element_type.157), channel_id=1, replica_groups=mesh['dp'=8,'expert'=64] {'expert'}, dimensions={0}, use_global_device_ids=true | all-gather | bytes 133120 | tf_op jit(solution)/shard_map/all_gather | solution.py:13
  116.5 21.4 %all-gather.3.cloned.1.call-done = bf16[64,16,64,128]{3,2,1,0:T(8,128)(2,1)} async-done(((bf16[1,16,64,128]{3,2,1,0:T(8,128)(2,1)}), bf16[64,16,64,128]{3,2,1,0:T(8,128)(2,1)}) %all-gather.3.cloned.1.call-update) | async-done | bytes 16777232 | tf_op jit(solution)/shard_map/all_gather | solution.py:13
  138.9 94.9 %while.20 = (s32[]{:T(128)}, f32[16,64,128]{2,1,0:T(8,128)S(1)}, f32[16,64]{1,0:T(8,128)S(1)}, f32[16,64]{1,0:T(8,128)S(1)}, bf16[64,16,64]{2,1,0:T(8,128)(2,1)S...) while((s32[]{:T(128)}, f32[16,64,128]{2,1,0:T(8,128)S(1)}, ...), condition=%wide.region_4.5_spmd, body=%wide.region_3.4_spmd.sunk | while | flops 532485 | bytes 1347735 | solution.py:25
  138.9 1.5 fusion.71
  140.4 1.5 fusion.71
  141.9 1.5 fusion.71
  143.5 1.5 fusion.71
  145.0 1.5 fusion.71
  146.5 1.5 fusion.71
  148.0 1.5 fusion.71
  149.5 1.5 fusion.71
  151.0 1.5 fusion.71
  152.5 1.5 fusion.71
  154.0 1.5 fusion.71
  155.5 1.5 fusion.71
  157.0 1.5 fusion.71
  158.5 1.5 fusion.71
  160.0 1.5 fusion.71
  161.5 1.5 fusion.71
  163.0 1.5 fusion.71
  164.5 1.5 fusion.71
  166.0 1.5 fusion.71
  167.5 1.5 fusion.71
  169.1 1.5 fusion.71
  170.6 1.5 fusion.71
  172.1 1.5 fusion.71
  173.6 1.5 fusion.71
  175.1 1.5 fusion.71
  176.6 1.5 fusion.71
  178.1 1.5 fusion.71
  179.6 1.5 fusion.71
  181.1 1.5 fusion.71
  182.6 1.5 fusion.71
  184.1 1.5 fusion.71
  185.6 1.5 fusion.71
  188.6 1.5 fusion.71
  191.6 1.5 fusion.71
  194.6 1.5 fusion.71
  196.2 1.5 fusion.71
  197.7 1.5 fusion.71
  199.2 1.5 fusion.71
  202.2 1.5 fusion.71
  205.2 1.5 fusion.71
  208.2 1.5 fusion.71
  211.2 1.5 fusion.71
  214.2 1.5 fusion.71
  217.2 1.5 fusion.71
  220.2 1.5 fusion.71
  223.3 1.5 fusion.71
  224.8 1.5 fusion.71
  226.3 1.5 fusion.71
  227.8 1.5 fusion.71
  230.8 1.5 fusion.71
  235.8 181.4 %all-reduce.4.cloned.1.call-done = f32[16,4096]{1,0:T(8,128)} async-done(((f32[16,4096]{1,0:T(8,128)}), f32[16,4096]{1,0:T(8,128)}) %all-reduce.4.cloned.1.call-update) | async-done | bytes 262160 | tf_op jit(solution)/shard_map/psum | solution.py:130
  419.4 26.8 %all-gather = bf16[8,4,4096]{2,1,0:T(4,128)(2,1)S(1)} all-gather(bf16[1,4,4096]{2,1,0:T(4,128)(2,1)S(1)} %fusion.3), channel_id=1, replica_groups=mesh['dp'=8,'expert'=64] {'dp'}, dimensions={0}, use_global_device_ids=true | all-gather | bytes 294912 | tf_op jit(solution)/shard_map/all_gather | solution.py:153
  446.3 1.5 fusion.10
  447.8 2.5 convolution_convert_fusion
  452.3 75.5 %all-reduce.6.cloned.1.call-done = bf16[32,4096]{1,0:T(8,128)(2,1)} async-done(((bf16[32,4096]{1,0:T(8,128)(2,1)}), bf16[32,4096]{1,0:T(8,128)(2,1)}) %all-reduce.6.cloned.1.call-update) | async-done | bytes 262160
  527.8 3.4 convolution_bitcast_fusion
  532.6 146.4 %reduce-scatter.4.cloned.1.call-done = f32[64,16]{1,0:T(8,128)} async-done(((f32[4096,16]{1,0:T(8,128)}), f32[64,16]{1,0:T(8,128)}) %reduce-scatter.4.cloned.1.call-update) | async-done | bytes 4112
  (148 shorter events, 44.1 us)
Async XLA Ops:
  7.2 440.7 %copy-start = (bf16[1,128,4096]{2,1,0:T(8,128)(2,1)S(1)}, bf16[1,128,4096]{2,1,0:T(8,128)(2,1)}, u32[]{:S(2)}) copy-start(bf16[1,128,4096]{2,1,0:T(8,128)(2,1)} %param.31) | copy-start | bytes 3145732
  7.2 227.1 %copy-start.1 = (bf16[128,4096]{1,0:T(8,128)(2,1)S(1)}, bf16[128,4096]{1,0:T(8,128)(2,1)}, u32[]{:S(2)}) copy-start(bf16[128,4096]{1,0:T(8,128)(2,1)} %param.25) | copy-start | bytes 3145732
  7.2 410.0 %copy-start.2 = (bf16[16,4096]{1,0:T(8,128)(2,1)S(1)}, bf16[16,4096]{1,0:T(8,128)(2,1)}, u32[]{:S(2)}) copy-start(bf16[16,4096]{1,0:T(8,128)(2,1)} %param.26) | copy-start | bytes 393220
  7.2 228.2 %copy-start.3 = (f32[128,8]{0,1:T(8,128)S(1)}, f32[128,8]{0,1:T(8,128)}, u32[]{:S(2)}) copy-start(f32[128,8]{0,1:T(8,128)} %param.28) | copy-start | bytes 12292
  11.2 22.2 %all-to-all-start = ((bf16[8,16,1024]{2,1,0:T(8,128)(2,1)}), bf16[8,16,1024]{2,1,0:T(8,128)(2,1)S(1)}, u32[]{:S(2)}, u32[]{:S(2)}) async-start(bf16[8,16,1024]{2,1,0:T(8,128)(2,1)} %broadcast_select_fusion), calls=%async_computation | async-start | bytes 524288 | tf_op jit(solution)/shard_map/all_to_all | solution.py:78
  21.6 116.3 %all-gather.3.cloned.1.call-start = ((), (), s32[]{:S(2)}) async-start(), calls=%async_computation.2 | async-start | bytes 17039360 | tf_op jit(solution)/shard_map/all_gather | solution.py:13
  36.8 380.4 %all-reduce.4.cloned.1.call-start = ((), (), s32[]{:S(2)}) async-start(), calls=%async_computation.3 | async-start | bytes 524288 | tf_op jit(solution)/shard_map/psum | solution.py:130
  235.3 292.4 %all-reduce.6.cloned.1.call-start = ((), (), s32[]{:S(2)}) async-start(), calls=%async_computation.5 | async-start | bytes 524288
  450.3 228.7 %reduce-scatter.4.cloned.1.call-start = ((), (), s32[]{:S(2)}) async-start(), calls=%async_computation.4 | async-start | bytes 2129920
Sparse Core Ops, SparseCore 0:
  36.9 100.9 all-gather.2
  235.5 181.6 all-reduce.3
  450.4 77.2 all-reduce.5
  532.3 146.7 reduce-scatter.3
where the time goes:
time: 690 us; the launch traced here: 687 us
  waiting for transfers between devices  431 us (62%)
  blocking collectives  103 us (15%)
  other arithmetic  100 us (14%)
  between operations  14.7 us (2%)
  local copies, waits for them, and re-layouts  13.4 us (2%)
  matrix products  11.9 us (2%)
  starting transfers between devices  10.5 us (2%)
    unnamed x6, waiting for transfers between devices  222 us
    psum x1, waiting for transfers between devices, shards(): projected = lax.psum(proj_terms, 'expert')  181 us
    add x63, other arithmetic, combine_parts(): out_first * factor_first[..., None] + out_second * factor_second[..., None]  91.5 us
    all_gather x2, blocking collectives, combined_all(): lax.all_gather(a.astype(kind), axis)  76.4 us
    all_gather x1, blocking collectives, shards(): piece = lax.all_gather(routed, 'dp', axis=0, tiled=True)  26.8 us
    all_gather x1, waiting for transfers between devices, combined_all(): lax.all_gather(a.astype(kind), axis)  21.4 us
  transfers between devices with their start and end apart: 5, of which 5 were waited for; matrix products, arithmetic and copies ran while one was open for 2% of the time, Pallas kernels for 0%

commit v1 on v0

--- a/solution.py
+++ b/solution.py
@@ -127,7 +127,8 @@
     ) / denominator[..., None]
     attended = attended.astype(jnp.bfloat16).reshape(local_rows, own_heads * HD)
     proj_terms = jnp.dot(attended, out_weight, preferred_element_type=jnp.float32)
-    projected = lax.psum(proj_terms, "expert")
+    order_ends = lambda inputs: jnp.sum(jax.lax.all_gather(inputs, axis_name="expert"), axis=0)
+    projected = order_ends(proj_terms)
     stream = residual.astype(jnp.float32) + projected
     inverse = lax.rsqrt(jnp.sum(stream * stream, axis=1, keepdims=True) / model_width + 1e-06)
     normed = (stream * inverse).astype(jnp.bfloat16)

time: 690 us -> 612 us (0.89)
  waiting for transfers between devices: 431 us -> 351 us
    psum x1 -> x0, waiting for transfers between devices: 181 us -> none  [shards(): projected = lax.psum(proj_terms, 'expert')]
    all_gather x0 -> x1, waiting for transfers between devices: none -> 102 us  [shards(): jax.lax.all_gather(inputs, axis_name='expert')]
where the time goes in v1:
time: 612 us; the launch traced here: 610 us
  waiting for transfers between devices  351 us (57%)
  other arithmetic  105 us (17%)
  blocking collectives  103 us (17%)
  between operations  14.7 us (2%)
  local copies, waits for them, and re-layouts  12.7 us (2%)
  starting transfers between devices  10.5 us (2%)
  matrix products  9.78 us (2%)
    unnamed x6, waiting for transfers between devices  221 us
    all_gather x1, waiting for transfers between devices, shards(): jax.lax.all_gather(inputs, axis_name='expert')  102 us
    add x63, other arithmetic, combine_parts(): out_first * factor_first[..., None] + out_second * factor_second[..., None]  91.5 us
    all_gather x2, blocking collectives, combined_all(): lax.all_gather(a.astype(kind), axis)  76.4 us
    all_gather x1, blocking collectives, shards(): piece = lax.all_gather(routed, 'dp', axis=0, tiled=True)  26.8 us
    all_gather x1, waiting for transfers between devices, combined_all(): lax.all_gather(a.astype(kind), axis)  22.6 us
  transfers between devices with their start and end apart: 5, of which 5 were waited for; matrix products, arithmetic and copies ran while one was open for 2% of the time, Pallas kernels for 0%

profile of v1, /device:TPU:16, one launch (start us, length us, event | category | flops | bytes accessed | tf_op | source)
XLA Modules:
  0.0 609.6 jit_solution(8140369422938496428)
XLA Ops:
  11.2 10.3 %all-to-all-start = ((bf16[8,16,1024]{2,1,0:T(8,128)(2,1)}), bf16[8,16,1024]{2,1,0:T(8,128)(2,1)S(1)}, u32[]{:S(2)}, u32[]{:S(2)}) async-start(bf16[8,16,1024]{2,1,0:T(8,128)(2,1)} %broadcast_select_fusion), calls=%async_computation | async-start | bytes 524288 | tf_op jit(solution)/shard_map/all_to_all | solution.py:78
  24.8 1.7 copy.82
  27.3 6.2 %all-to-all-done = bf16[8,16,1024]{2,1,0:T(8,128)(2,1)S(1)} async-done(((bf16[8,16,1024]{2,1,0:T(8,128)(2,1)}), bf16[8,16,1024]{2,1,0:T(8,128)(2,1)S(1)}, u32[]{:S(2)}, u32[]{:S(2)}) %all-to-all-start) | async-done | bytes 262176 | tf_op jit(solution)/shard_map/all_to_all | solution.py:78
  38.8 39.2 %all_gather.23 = bf16[64,16,64]{2,1,0:T(8,128)(2,1)S(1)} all-gather(bf16[1,16,64]{2,1,0:T(8,128)(2,1)S(1)} %convert_element_type.161), channel_id=1, replica_groups=mesh['dp'=8,'expert'=64] {'expert'}, dimensions={0}, use_global_device_ids=true | all-gather | bytes 133120 | tf_op jit(solution)/shard_map/all_gather | solution.py:13
  78.1 37.2 %all_gather.22 = bf16[64,16,64]{2,1,0:T(8,128)(2,1)S(1)} all-gather(bf16[1,16,64]{2,1,0:T(8,128)(2,1)S(1)} %convert_element_type.157), channel_id=1, replica_groups=mesh['dp'=8,'expert'=64] {'expert'}, dimensions={0}, use_global_device_ids=true | all-gather | bytes 133120 | tf_op jit(solution)/shard_map/all_gather | solution.py:13
  115.3 22.6 %all-gather.5.cloned.1.call-done = bf16[64,16,64,128]{3,2,1,0:T(8,128)(2,1)} async-done(((bf16[1,16,64,128]{3,2,1,0:T(8,128)(2,1)}), bf16[64,16,64,128]{3,2,1,0:T(8,128)(2,1)}) %all-gather.5.cloned.1.call-update) | async-done | bytes 16777232 | tf_op jit(solution)/shard_map/all_gather | solution.py:13
  138.9 94.9 %while.20 = (s32[]{:T(128)}, f32[16,64,128]{2,1,0:T(8,128)S(1)}, f32[16,64]{1,0:T(8,128)S(1)}, f32[16,64]{1,0:T(8,128)S(1)}, bf16[64,16,64]{2,1,0:T(8,128)(2,1)S...) while((s32[]{:T(128)}, f32[16,64,128]{2,1,0:T(8,128)S(1)}, ...), condition=%wide.region_4.5_spmd, body=%wide.region_3.4_spmd.sunk | while | flops 532485 | bytes 1347735 | solution.py:25
  138.9 1.5 fusion.71
  140.4 1.5 fusion.71
  142.0 1.5 fusion.71
  143.5 1.5 fusion.71
  145.0 1.5 fusion.71
  146.5 1.5 fusion.71
  148.0 1.5 fusion.71
  149.5 1.5 fusion.71
  151.0 1.5 fusion.71
  152.5 1.5 fusion.71
  154.0 1.5 fusion.71
  155.5 1.5 fusion.71
  157.0 1.5 fusion.71
  158.5 1.5 fusion.71
  160.0 1.5 fusion.71
  161.5 1.5 fusion.71
  163.0 1.5 fusion.71
  164.5 1.5 fusion.71
  166.0 1.5 fusion.71
  167.5 1.5 fusion.71
  169.1 1.5 fusion.71
  170.6 1.5 fusion.71
  172.1 1.5 fusion.71
  173.6 1.5 fusion.71
  175.1 1.5 fusion.71
  176.6 1.5 fusion.71
  178.1 1.5 fusion.71
  179.6 1.5 fusion.71
  181.1 1.5 fusion.71
  182.6 1.5 fusion.71
  184.1 1.5 fusion.71
  185.6 1.5 fusion.71
  187.1 1.5 fusion.71
  188.6 1.5 fusion.71
  191.6 1.5 fusion.71
  194.7 1.5 fusion.71
  197.7 1.5 fusion.71
  200.7 1.5 fusion.71
  203.7 1.5 fusion.71
  205.2 1.5 fusion.71
  206.7 1.5 fusion.71
  208.2 1.5 fusion.71
  211.2 1.5 fusion.71
  214.2 1.5 fusion.71
  217.2 1.5 fusion.71
  220.3 1.5 fusion.71
  223.3 1.5 fusion.71
  226.3 1.5 fusion.71
  229.3 1.5 fusion.71
  232.3 1.5 fusion.71
  236.3 101.5 %all-gather.7.cloned.1.call-done = f32[1024,4096]{1,0:T(8,128)} async-done(((f32[16,4096]{1,0:T(8,128)}), f32[1024,4096]{1,0:T(8,128)}) %all-gather.7.cloned.1.call-update) | async-done | bytes 16777232 | tf_op jit(solution)/shard_map/all_gather | solution.py:130
  337.8 6.6 %reduce_sum.56 = f32[16,4096]{1,0:T(8,128)S(1)} reduce(f32[64,16,4096]{2,1,0:T(8,128)} %bitcast.98, f32[]{:T(128)} %constant.124.clone.1), dimensions={0}, to_apply=%region_6.8 | reduce | flops 4128768 | bytes 17039364 | tf_op jit(solution)/shard_map/reduce_sum | solution.py:130
  344.8 26.8 %all-gather.1 = bf16[8,4,4096]{2,1,0:T(4,128)(2,1)S(1)} all-gather(bf16[1,4,4096]{2,1,0:T(4,128)(2,1)S(1)} %fusion.3), channel_id=1, replica_groups=mesh['dp'=8,'expert'=64] {'dp'}, dimensions={0}, use_global_device_ids=true | all-gather | bytes 294912 | tf_op jit(solution)/shard_map/all_gather | solution.py:154
  371.9 2.5 convolution_convert_fusion
  376.4 73.3 %all-reduce.3.cloned.1.call-done = bf16[32,4096]{1,0:T(8,128)(2,1)} async-done(((bf16[32,4096]{1,0:T(8,128)(2,1)}), bf16[32,4096]{1,0:T(8,128)(2,1)}) %all-reduce.3.cloned.1.call-update) | async-done | bytes 262160
  449.7 3.4 convolution_bitcast_fusion
  453.8 147.8 %reduce-scatter.4.cloned.1.call-done = f32[64,16]{1,0:T(8,128)} async-done(((f32[4096,16]{1,0:T(8,128)}), f32[64,16]{1,0:T(8,128)}) %reduce-scatter.4.cloned.1.call-update) | async-done | bytes 4112
  (153 shorter events, 41.1 us)
Async XLA Ops:
  7.2 364.8 %copy-start = (bf16[1,128,4096]{2,1,0:T(8,128)(2,1)S(1)}, bf16[1,128,4096]{2,1,0:T(8,128)(2,1)}, u32[]{:S(2)}) copy-start(bf16[1,128,4096]{2,1,0:T(8,128)(2,1)} %param.31) | copy-start | bytes 3145732
  7.2 227.1 %copy-start.1 = (bf16[128,4096]{1,0:T(8,128)(2,1)S(1)}, bf16[128,4096]{1,0:T(8,128)(2,1)}, u32[]{:S(2)}) copy-start(bf16[128,4096]{1,0:T(8,128)(2,1)} %param.25) | copy-start | bytes 3145732
  7.2 228.2 %copy-start.4 = (s32[128,8]{0,1:T(8,128)S(1)}, s32[128,8]{0,1:T(8,128)}, u32[]{:S(2)}) copy-start(s32[128,8]{0,1:T(8,128)} %param.27) | copy-start | bytes 12292
  7.2 228.9 %copy-start.5 = (f32[128,8]{0,1:T(8,128)S(1)}, f32[128,8]{0,1:T(8,128)}, u32[]{:S(2)}) copy-start(f32[128,8]{0,1:T(8,128)} %param.28) | copy-start | bytes 12292
  11.2 22.2 %all-to-all-start = ((bf16[8,16,1024]{2,1,0:T(8,128)(2,1)}), bf16[8,16,1024]{2,1,0:T(8,128)(2,1)S(1)}, u32[]{:S(2)}, u32[]{:S(2)}) async-start(bf16[8,16,1024]{2,1,0:T(8,128)(2,1)} %broadcast_select_fusion), calls=%async_computation | async-start | bytes 524288 | tf_op jit(solution)/shard_map/all_to_all | solution.py:78
  21.5 116.4 %all-gather.5.cloned.1.call-start = ((), (), s32[]{:S(2)}) async-start(), calls=%async_computation.2 | async-start | bytes 17039360 | tf_op jit(solution)/shard_map/all_gather | solution.py:13
  33.5 310.9 %copy-start.3 = (bf16[16,4096]{1,0:T(8,128)(2,1)S(1)}, bf16[16,4096]{1,0:T(8,128)(2,1)}, u32[]{:S(2)}) copy-start(bf16[16,4096]{1,0:T(8,128)(2,1)} %param.26) | copy-start | bytes 393220
  36.8 301.1 %all-gather.7.cloned.1.call-start = ((), (), s32[]{:S(2)}) async-start(), calls=%async_computation.3 | async-start | bytes 17039360 | tf_op jit(solution)/shard_map/all_gather | solution.py:130
  235.3 136.3 %copy-start.2 = (bf16[1,4096,128]{2,1,0:T(8,128)(2,1)S(1)}, bf16[1,4096,128]{2,1,0:T(8,128)(2,1)}, u32[]{:S(2)}) copy-start(bf16[1,4096,128]{2,1,0:T(8,128)(2,1)} %param.29) | copy-start | bytes 3145732
  235.3 214.4 %all-reduce.3.cloned.1.call-start = ((), (), s32[]{:S(2)}) async-start(), calls=%async_computation.5 | async-start | bytes 524288
  374.4 227.2 %reduce-scatter.4.cloned.1.call-start = ((), (), s32[]{:S(2)}) async-start(), calls=%async_computation.4 | async-start | bytes 2129920
Sparse Core Ops, SparseCore 0:
  36.9 100.9 all-gather.4
  235.5 102.3 all-gather.6
  374.6 75.1 all-reduce.2
  454.9 146.6 reduce-scatter.3
